TPU v7x, 512 devices: a whole 4x4x16 slice. The times are simulated.
512 devices in a mesh: row: 32 (over z, core), col: 16 (over y, x).
Axes of the slice: x: 4, y: 4, z: 16, core: 2. Of those that a mesh axis runs over, the one named last changes fastest.
Arguments:
- pressure_in: float32 [1024, 256, 128], P('row', 'col'), may hold values from -6 to 6
- source: float32 [1024, 256, 128], P('row', 'col'), may hold values from -18 to 18
- permeability: float32 [1024, 256, 128], P('row', 'col'), may hold values from 0.2 to 5
Outputs:
- pressure_out: float32 [1024, 256, 128], P('row', 'col')
All inputs are finite; a program needn't handle non-finite values.
Results may differ from a plain program's by a relative error of at most 0.0001.
Values sent between devices are 32-bit elements; how exact they have to be, the bound alone decides.
No kernel may reach another device: no remote copies, remote signals or barrier semaphores. Data moves between devices by JAX's collectives and lax.ppermute only.
A program may use at most 128 MiB of HBM per device.

v0:
```python
import jax
import jax.numpy as jnp
from jax import lax
from jax.sharding import PartitionSpec as P

LEVELS = 3
NU1 = 2
NU2 = 2
CSWEEPS = 16
OMEGA = 0.8


def padded_2(array, sides, width):
    for axis, dim in sides:
        size, length = (lax.axis_size(axis), array.shape[dim])
        up = [(i, (i + 1) % size) for i in range(size)]
        down = [(j, i) for i, j in up]
        last = lax.slice_in_dim(array, length - width, length, axis=dim)
        first = lax.slice_in_dim(array, 0, width, axis=dim)
        before = lax.ppermute(last, axis, up)
        after = lax.ppermute(first, axis, down)
        array = jnp.concatenate([before, array, after], axis=dim)
    return array


def harmonic(left, right, scale):
    return 2.0 * left * right / (left + right) * scale


def coefficients(padded, center, scale):
    west_x = harmonic(padded[:-2, 1:-1], center, scale)
    east_x = harmonic(center, padded[2:, 1:-1], scale)
    west_y = harmonic(padded[1:-1, :-2], center, scale)
    east_y = harmonic(center, padded[1:-1, 2:], scale)
    inner = harmonic(center[:, :, :-1], center[:, :, 1:], scale)
    below = jnp.concatenate([2.0 * center[:, :, :1] * scale, inner], axis=2)
    above = jnp.concatenate([inner, 2.0 * center[:, :, -1:] * scale], axis=2)
    diagonal = west_x + east_x + west_y + east_y + below + above
    return (west_x, east_x, west_y, east_y, below, above, diagonal)


def apply_operator(padded, center, faces):
    west_x, east_x, west_y, east_y, below, above, diagonal = faces
    zero_plane = jnp.zeros_like(center[:, :, :1])
    under = jnp.concatenate([zero_plane, center[:, :, :-1]], axis=2)
    over = jnp.concatenate([center[:, :, 1:], zero_plane], axis=2)
    beside_all = west_x * padded[:-2, 1:-1] + east_x * padded[2:, 1:-1]
    beside_all = beside_all + west_y * padded[1:-1, :-2] + east_y * padded[1:-1, 2:]
    beside_all = beside_all + below * under + above * over
    return diagonal * center - beside_all


def jacobi_sweep(pressure, right_side, faces, padder):
    return (
        pressure
        + OMEGA * (right_side - apply_operator(padder(pressure), pressure, faces)) / faces[6]
    )


def first_sweep(right_side, faces):
    return OMEGA * right_side / faces[6]


def coarsen(field):
    size_x, size_y, size_z = field.shape
    return field.reshape(size_x // 2, 2, size_y // 2, 2, size_z // 2, 2).mean(axis=(1, 3, 5))


def prolong(field):
    return jnp.repeat(jnp.repeat(jnp.repeat(field, 2, axis=0), 2, axis=1), 2, axis=2)


def mesh_pad(field):
    return padded_2(field, (("row", 0), ("col", 1)), 1)


def perm_pad(field):
    return padded_2(field, (("row", 0), ("col", 1)), 1)


def band_pad(field):
    extended = padded_2(field, (("row", 0),), 1)
    return jnp.pad(extended, ((0, 0), (1, 1), (0, 0)), mode="wrap")


def band_perm_pad(field):
    extended = padded_2(field, (("row", 0),), 1)
    return jnp.pad(extended, ((0, 0), (1, 1), (0, 0)), mode="wrap")


def coarse_solve(right_side, faces, padder):
    start = first_sweep(right_side, faces)

    def one_sweep(sweep_index, current):
        return jacobi_sweep(current, right_side, faces, padder)

    return lax.fori_loop(1, CSWEEPS, one_sweep, start)


def on_device(pressure_in, source, permeability):
    perms = [permeability]
    for depth_level in range(LEVELS):
        perms.append(coarsen(perms[depth_level]))
    pressure = pressure_in
    right_side = source
    states = []
    all_faces = [
        coefficients(perm_pad(perms[depth_level]), perms[depth_level], 0.25**depth_level)
        for depth_level in range(LEVELS)
    ]
    for depth_level in range(LEVELS):
        faces = all_faces[depth_level]
        if depth_level == 0:
            for sweep_index in range(NU1):
                pressure = jacobi_sweep(pressure, right_side, faces, mesh_pad)
        else:
            pressure = first_sweep(right_side, faces)
            pressure = jacobi_sweep(pressure, right_side, faces, mesh_pad)
        states.append((pressure, right_side))
        residual = right_side - apply_operator(mesh_pad(pressure), pressure, faces)
        right_side = coarsen(residual)
    coarse_perm = perms[LEVELS]
    size_x, size_y, size_z = right_side.shape
    coarse_scale = 0.25**LEVELS
    band_rhs, band_perm = (
        lax.all_gather(right_side, "col", axis=1, tiled=True),
        lax.all_gather(coarse_perm, "col", axis=1, tiled=True),
    )
    band_faces = coefficients(band_perm_pad(band_perm), band_perm, coarse_scale)
    solved = coarse_solve(band_rhs, band_faces, band_pad)
    correction = lax.dynamic_slice_in_dim(solved, lax.axis_index("col") * size_y, size_y, 1)
    for depth_level in range(LEVELS - 1, -1, -1):
        pressure, right_side = states[depth_level]
        pressure = pressure + prolong(correction)
        for sweep_index in range(NU2):
            pressure = jacobi_sweep(pressure, right_side, all_faces[depth_level], mesh_pad)
        correction = pressure
    return correction


def solution(mesh):
    placed = (P("row", "col", None), P("row", "col", None), P("row", "col", None))
    return jax.shard_map(
        on_device, mesh=mesh, in_specs=placed, out_specs=P("row", "col", None), check_vma=False
    )
```

profile of v0, /device:TPU:30, one launch (start us, length us, event | category | flops | bytes accessed | tf_op | source)
XLA Modules:
  0.0 433.4 jit_solution(4026333652085899989)
XLA Ops:
  0.7 8.9 %collective-permute-start.3 = (f32[1,16,128]{2,1,0:T(8,128)S(1)}, f32[1,16,128]{2,1,0:T(8,128)S(1)}, u32[]{:S(2)}, u32[]{:S(2)}) collective-permute-start(f32[1,16,128]{2,1,0:T(8,128)S(1)} %get-tuple-element.177), channel_id=1, source_target_pairs={{16,0},{32,16},{48,32},{64,48},{80,64},{96,80},{112,96},{128,112},... | collective-permute-start | bytes 24584 | tf_op jit(solution)/shard_map/ppermute | solution.py:21
  10.4 3.0 collective-permute-start.7
  17.4 18.9 %reshape.48 = f32[16,2,8,2,64,2]{5,4,3,2,1,0:T(8,128)} reshape(f32[32,16,128]{2,1,0:T(8,128)} %param.7) | data formatting | bytes 524288 | tf_op jit(solution)/shard_map/reshape | solution.py:66
  36.4 7.0 %reduce_sum.55 = f32[16,8,64]{2,1,0:T(8,128)S(1)} reduce(f32[16,2,8,2,64,2]{5,4,3,2,1,0:T(8,128)} %reshape.48, f32[]{:T(128)} %constant.23.clone.1), dimensions={1,3,5}, to_apply=%region_1.0 | reduce | flops 57344 | bytes 294916 | tf_op jit(solution)/shard_map/reduce_sum | solution.py:66
  48.9 21.4 %all_gather.7 = f32[4,32,16]{2,0,1:T(4,128)S(1)} all-gather(f32[4,2,16]{2,0,1:T(4,128)S(1)} %broadcast_multiply_fusion.2), channel_id=1, replica_groups=mesh['row'=32,'col'=16] {'col'}, dimensions={1}, use_global_device_ids=true | all-gather | bytes 8704 | tf_op jit(solution)/shard_map/all_gather | solution.py:127
  71.7 4.7 %collective-permute-start.4 = (f32[34,1,128]{2,1,0:T(1,128)S(1)}, f32[34,1,128]{2,1,0:T(1,128)S(1)}, u32[]{:S(2)}, u32[]{:S(2)}) collective-permute-start(f32[34,1,128]{2,1,0:T(1,128)S(1)} %get-tuple-element.156), channel_id=1, source_target_pairs={{0,1},{1,2},{2,3},{3,4},{4,5},{5,6},{6,7},{7,8},{8,9},{9,10},{10,1... | collective-permute-start | bytes 52232 | tf_op jit(solution)/shard_map/ppermute | solution.py:20
  78.4 7.2 %collective-permute-start.8 = (f32[34,1,128]{2,1,0:T(1,128)S(1)}, f32[34,1,128]{2,1,0:T(1,128)S(1)}, u32[]{:S(2)}, u32[]{:S(2)}) collective-permute-start(f32[34,1,128]{2,1,0:T(1,128)S(1)} %get-tuple-element.157), channel_id=1, source_target_pairs={{0,1},{1,2},{2,3},{3,4},{4,5},{5,6},{6,7},{7,8},{8,9},{9,10},{10,1... | collective-permute-start | bytes 52232 | tf_op jit(solution)/shard_map/ppermute | solution.py:20
  90.6 4.0 collective-permute-done.9
  96.7 2.9 collective-permute-start.11
  101.0 3.2 collective-permute-start.12
  110.0 3.2 collective-permute-done.13
  118.7 3.3 collective-permute-start.16
  124.7 6.6 %collective-permute-start.20 = (f32[18,1,64]{2,1,0:T(1,128)S(1)}, f32[18,1,64]{2,1,0:T(1,128)S(1)}, u32[]{:S(2)}, u32[]{:S(2)}) collective-permute-start(f32[18,1,64]{2,1,0:T(1,128)S(1)} %get-tuple-element.192), channel_id=1, source_target_pairs={{0,1},{1,2},{2,3},{3,4},{4,5},{5,6},{6,7},{7,8},{8,9},{9,10},{10,1... | collective-permute-start | bytes 13832 | tf_op jit(solution)/shard_map/ppermute | solution.py:20
  134.4 18.1 %reshape.47 = f32[16,2,8,2,64,2]{5,4,3,2,1,0:T(8,128)} reshape(f32[32,16,128]{2,1,0:T(8,128)S(1)} %fusion.47) | data formatting | bytes 524288 | tf_op jit(solution)/shard_map/reshape | solution.py:66
  152.5 7.0 %reduce_sum.54 = f32[16,8,64]{2,1,0:T(8,128)S(1)} reduce(f32[16,2,8,2,64,2]{5,4,3,2,1,0:T(8,128)} %reshape.47, f32[]{:T(128)} %constant.23.clone.1), dimensions={1,3,5}, to_apply=%region_0.0 | reduce | flops 57344 | bytes 294916 | tf_op jit(solution)/shard_map/reduce_sum | solution.py:66
  159.8 2.9 collective-permute-start.23
  164.1 7.2 %collective-permute-start.24 = (f32[18,1,64]{2,1,0:T(1,128)S(1)}, f32[18,1,64]{2,1,0:T(1,128)S(1)}, u32[]{:S(2)}, u32[]{:S(2)}) collective-permute-start(f32[18,1,64]{2,1,0:T(1,128)S(1)} %get-tuple-element.189), channel_id=1, source_target_pairs={{0,1},{1,2},{2,3},{3,4},{4,5},{5,6},{6,7},{7,8},{8,9},{9,10},{10,1... | collective-permute-start | bytes 13832 | tf_op jit(solution)/shard_map/ppermute | solution.py:20
  173.3 2.9 collective-permute-start.43
  176.3 3.9 collective-permute-done.25
  184.7 3.3 collective-permute-start.28
  190.6 6.7 %collective-permute-start.32 = (f32[10,1,32]{2,1,0:T(1,128)}, f32[10,1,32]{2,1,0:T(1,128)}, u32[]{:S(2)}, u32[]{:S(2)}) collective-permute-start(f32[10,1,32]{2,1,0:T(1,128)} %get-tuple-element.228), channel_id=1, source_target_pairs={{0,1},{1,2},{2,3},{3,4},{4,5},{5,6},{6,7},{7,8},{8,9},{9,10},{10,1... | collective-permute-start | bytes 3848 | tf_op jit(solution)/shard_map/ppermute | solution.py:20
  200.3 3.0 reshape.49
  207.4 2.9 collective-permute-start.35
  211.7 4.9 %collective-permute-start.36 = (f32[10,1,32]{2,1,0:T(1,128)S(1)}, f32[10,1,32]{2,1,0:T(1,128)S(1)}, u32[]{:S(2)}, u32[]{:S(2)}) collective-permute-start(f32[10,1,32]{2,1,0:T(1,128)S(1)} %get-tuple-element.225), channel_id=1, source_target_pairs={{0,1},{1,2},{2,3},{3,4},{4,5},{5,6},{6,7},{7,8},{8,9},{9,10},{10,1... | collective-permute-start | bytes 3848 | tf_op jit(solution)/shard_map/ppermute | solution.py:20
  218.6 6.8 %collective-permute-done.37 = f32[10,1,32]{2,1,0:T(1,128)S(1)} collective-permute-done((f32[10,1,32]{2,1,0:T(1,128)S(1)}, f32[10,1,32]{2,1,0:T(1,128)S(1)}, u32[]{:S(2)}, u32[]{:S(2)}) %collective-permute-start.37) | collective-permute-done | bytes 1312 | tf_op jit(solution)/shard_map/ppermute | solution.py:21
  226.3 2.9 collective-permute-start.39
  232.5 3.9 collective-permute-start.41
  236.5 4.8 %collective-permute-done.41 = f32[10,1,32]{2,1,0:T(1,128)S(1)} collective-permute-done((f32[10,1,32]{2,1,0:T(1,128)S(1)}, f32[10,1,32]{2,1,0:T(1,128)S(1)}, u32[]{:S(2)}, u32[]{:S(2)}) %collective-permute-start.41) | collective-permute-done | bytes 1312 | tf_op jit(solution)/shard_map/ppermute | solution.py:21
  242.4 20.3 %all_gather.6 = f32[4,32,16]{2,0,1:T(4,128)S(1)} all-gather(f32[4,2,16]{2,0,1:T(4,128)S(1)} %broadcast_multiply_fusion.3), channel_id=1, replica_groups=mesh['row'=32,'col'=16] {'col'}, dimensions={1}, use_global_device_ids=true | all-gather | bytes 8704 | tf_op jit(solution)/shard_map/all_gather | solution.py:126
  263.9 68.6 %while.10 = (s32[]{:T(128)}, f32[4,32,16]{1,2,0:T(8,128)S(1)}, f32[4,32,16]{1,2,0:T(8,128)S(1)}, f32[4,32,16]{1,2,0:T(8,128)S(1)}, f32[4,32,16]{1,2,0:T(8,128)S(...) while((s32[]{:T(128)}, f32[4,32,16]{1,2,0:T(8,128)S(1)}, ...), condition=%wide.region_7.8_spmd, body=%wide.region_6.7_spmd.sunk | while | flops 43010 | bytes 279997 | solution.py:97
  264.0 2.9 collective-permute-start.1
  268.5 2.9 collective-permute-start.1
  273.1 2.9 collective-permute-start.1
  277.7 2.9 collective-permute-start.1
  282.3 2.9 collective-permute-start.1
  286.8 2.9 collective-permute-start.1
  337.2 4.9 %collective-permute-start.46 = (f32[10,1,32]{2,1,0:T(1,128)S(1)}, f32[10,1,32]{2,1,0:T(1,128)S(1)}, u32[]{:S(2)}, u32[]{:S(2)}) collective-permute-start(f32[10,1,32]{2,1,0:T(1,128)S(1)} %get-tuple-element.221), channel_id=1, source_target_pairs={{0,1},{1,2},{2,3},{3,4},{4,5},{5,6},{6,7},{7,8},{8,9},{9,10},{10,1... | collective-permute-start | bytes 3848 | tf_op jit(solution)/shard_map/ppermute | solution.py:20
  344.1 6.8 %collective-permute-done.47 = f32[10,1,32]{2,1,0:T(1,128)S(1)} collective-permute-done((f32[10,1,32]{2,1,0:T(1,128)S(1)}, f32[10,1,32]{2,1,0:T(1,128)S(1)}, u32[]{:S(2)}, u32[]{:S(2)}) %collective-permute-start.47) | collective-permute-done | bytes 1312 | tf_op jit(solution)/shard_map/ppermute | solution.py:21
  357.9 3.9 collective-permute-start.51
  362.0 4.8 %collective-permute-done.51 = f32[10,1,32]{2,1,0:T(1,128)S(1)} collective-permute-done((f32[10,1,32]{2,1,0:T(1,128)S(1)}, f32[10,1,32]{2,1,0:T(1,128)S(1)}, u32[]{:S(2)}, u32[]{:S(2)}) %collective-permute-start.51) | collective-permute-done | bytes 1312 | tf_op jit(solution)/shard_map/ppermute | solution.py:21
  374.2 3.9 collective-permute-start.55
  378.2 4.9 %collective-permute-done.55 = f32[18,1,64]{2,1,0:T(1,128)S(1)} collective-permute-done((f32[18,1,64]{2,1,0:T(1,128)S(1)}, f32[18,1,64]{2,1,0:T(1,128)S(1)}, u32[]{:S(2)}, u32[]{:S(2)}) %collective-permute-start.55) | collective-permute-done | bytes 4640 | tf_op jit(solution)/shard_map/ppermute | solution.py:21
  390.5 3.9 collective-permute-start.59
  394.5 4.9 %collective-permute-done.59 = f32[18,1,64]{2,1,0:T(1,128)S(1)} collective-permute-done((f32[18,1,64]{2,1,0:T(1,128)S(1)}, f32[18,1,64]{2,1,0:T(1,128)S(1)}, u32[]{:S(2)}, u32[]{:S(2)}) %collective-permute-start.59) | collective-permute-done | bytes 4640 | tf_op jit(solution)/shard_map/ppermute | solution.py:21
  407.7 3.9 collective-permute-start.63
  411.8 4.9 %collective-permute-done.63 = f32[34,1,128]{2,1,0:T(1,128)S(1)} collective-permute-done((f32[34,1,128]{2,1,0:T(1,128)S(1)}, f32[34,1,128]{2,1,0:T(1,128)S(1)}, u32[]{:S(2)}, u32[]{:S(2)}) %collective-permute-start.63) | collective-permute-done | bytes 17440 | tf_op jit(solution)/shard_map/ppermute | solution.py:21
  423.4 3.9 collective-permute-start.67
  427.5 4.9 %collective-permute-done.67 = f32[34,1,128]{2,1,0:T(1,128)S(1)} collective-permute-done((f32[34,1,128]{2,1,0:T(1,128)S(1)}, f32[34,1,128]{2,1,0:T(1,128)S(1)}, u32[]{:S(2)}, u32[]{:S(2)}) %collective-permute-start.67) | collective-permute-done | bytes 17440 | tf_op jit(solution)/shard_map/ppermute | solution.py:21
  (441 shorter events, 161.8 us)
Async XLA Ops:
  0.7 70.9 %collective-permute-start.2 = (f32[1,16,128]{2,1,0:T(8,128)S(1)}, f32[1,16,128]{2,1,0:T(8,128)S(1)}, u32[]{:S(2)}, u32[]{:S(2)}) collective-permute-start(f32[1,16,128]{2,1,0:T(8,128)S(1)} %get-tuple-element.178), channel_id=1, source_target_pairs={{0,16},{16,32},{32,48},{48,64},{64,80},{80,96},{96,112},{112,128},... | collective-permute-start | bytes 24584 | tf_op jit(solution)/shard_map/ppermute | solution.py:20
  0.7 70.9 %collective-permute-start.3 = (f32[1,16,128]{2,1,0:T(8,128)S(1)}, f32[1,16,128]{2,1,0:T(8,128)S(1)}, u32[]{:S(2)}, u32[]{:S(2)}) collective-permute-start(f32[1,16,128]{2,1,0:T(8,128)S(1)} %get-tuple-element.177), channel_id=1, source_target_pairs={{16,0},{32,16},{48,32},{64,48},{80,64},{96,80},{112,96},{128,112},... | collective-permute-start | bytes 24584 | tf_op jit(solution)/shard_map/ppermute | solution.py:21
  10.4 67.9 %collective-permute-start.6 = (f32[1,16,128]{2,1,0:T(8,128)S(1)}, f32[1,16,128]{2,1,0:T(8,128)S(1)}, u32[]{:S(2)}, u32[]{:S(2)}) collective-permute-start(f32[1,16,128]{2,1,0:T(8,128)S(1)} %get-tuple-element.182), channel_id=1, source_target_pairs={{0,16},{16,32},{32,48},{48,64},{64,80},{80,96},{96,112},{112,128},... | collective-permute-start | bytes 24584 | tf_op jit(solution)/shard_map/ppermute | solution.py:20
  10.4 68.0 %collective-permute-start.7 = (f32[1,16,128]{2,1,0:T(8,128)S(1)}, f32[1,16,128]{2,1,0:T(8,128)S(1)}, u32[]{:S(2)}, u32[]{:S(2)}) collective-permute-start(f32[1,16,128]{2,1,0:T(8,128)S(1)} %get-tuple-element.181), channel_id=1, source_target_pairs={{16,0},{32,16},{48,32},{64,48},{80,64},{96,80},{112,96},{128,112},... | collective-permute-start | bytes 24584 | tf_op jit(solution)/shard_map/ppermute | solution.py:21
  71.7 16.0 %collective-permute-start.4 = (f32[34,1,128]{2,1,0:T(1,128)S(1)}, f32[34,1,128]{2,1,0:T(1,128)S(1)}, u32[]{:S(2)}, u32[]{:S(2)}) collective-permute-start(f32[34,1,128]{2,1,0:T(1,128)S(1)} %get-tuple-element.156), channel_id=1, source_target_pairs={{0,1},{1,2},{2,3},{3,4},{4,5},{5,6},{6,7},{7,8},{8,9},{9,10},{10,1... | collective-permute-start | bytes 52232 | tf_op jit(solution)/shard_map/ppermute | solution.py:20
  76.4 14.2 %collective-permute-start.5 = (f32[34,1,128]{2,1,0:T(1,128)S(1)}, f32[34,1,128]{2,1,0:T(1,128)S(1)}, u32[]{:S(2)}, u32[]{:S(2)}) collective-permute-start(f32[34,1,128]{2,1,0:T(1,128)S(1)} %get-tuple-element.155), channel_id=1, source_target_pairs={{1,0},{2,1},{3,2},{4,3},{5,4},{6,5},{7,6},{8,7},{9,8},{10,9},{11,1... | collective-permute-start | bytes 52232 | tf_op jit(solution)/shard_map/ppermute | solution.py:21
  78.4 12.2 %collective-permute-start.8 = (f32[34,1,128]{2,1,0:T(1,128)S(1)}, f32[34,1,128]{2,1,0:T(1,128)S(1)}, u32[]{:S(2)}, u32[]{:S(2)}) collective-permute-start(f32[34,1,128]{2,1,0:T(1,128)S(1)} %get-tuple-element.157), channel_id=1, source_target_pairs={{0,1},{1,2},{2,3},{3,4},{4,5},{5,6},{6,7},{7,8},{8,9},{9,10},{10,1... | collective-permute-start | bytes 52232 | tf_op jit(solution)/shard_map/ppermute | solution.py:20
  85.7 9.0 %collective-permute-start.9 = (f32[34,1,128]{2,1,0:T(1,128)S(1)}, f32[34,1,128]{2,1,0:T(1,128)S(1)}, u32[]{:S(2)}, u32[]{:S(2)}) collective-permute-start(f32[34,1,128]{2,1,0:T(1,128)S(1)} %get-tuple-element.158), channel_id=1, source_target_pairs={{1,0},{2,1},{3,2},{4,3},{5,4},{6,5},{7,6},{8,7},{9,8},{10,9},{11,1... | collective-permute-start | bytes 52232 | tf_op jit(solution)/shard_map/ppermute | solution.py:21
  87.6 26.7 %collective-permute-start.18 = (f32[1,8,64]{2,1,0:T(8,128)S(1)}, f32[1,8,64]{2,1,0:T(8,128)S(1)}, u32[]{:S(2)}, u32[]{:S(2)}) collective-permute-start(f32[1,8,64]{2,1,0:T(8,128)S(1)} %get-tuple-element.212), channel_id=1, source_target_pairs={{0,16},{16,32},{32,48},{48,64},{64,80},{80,96},{96,112},{112,128},... | collective-permute-start | bytes 6152 | tf_op jit(solution)/shard_map/ppermute | solution.py:20
  87.7 29.7 %collective-permute-start.19 = (f32[1,8,64]{2,1,0:T(8,128)S(1)}, f32[1,8,64]{2,1,0:T(8,128)S(1)}, u32[]{:S(2)}, u32[]{:S(2)}) collective-permute-start(f32[1,8,64]{2,1,0:T(8,128)S(1)} %get-tuple-element.211), channel_id=1, source_target_pairs={{16,0},{32,16},{48,32},{64,48},{80,64},{96,80},{112,96},{128,112},... | collective-permute-start | bytes 6152 | tf_op jit(solution)/shard_map/ppermute | solution.py:21
  96.7 4.3 collective-permute-start.11
  101.0 6.0 %collective-permute-start.12 = (f32[34,1,128]{2,1,0:T(1,128)S(1)}, f32[34,1,128]{2,1,0:T(1,128)S(1)}, u32[]{:S(2)}, u32[]{:S(2)}) collective-permute-start(f32[34,1,128]{2,1,0:T(1,128)S(1)} %get-tuple-element.153), channel_id=1, source_target_pairs={{0,1},{1,2},{2,3},{3,4},{4,5},{5,6},{6,7},{7,8},{8,9},{9,10},{10,1... | collective-permute-start | bytes 52232 | tf_op jit(solution)/shard_map/ppermute | solution.py:20
  104.3 9.0 %collective-permute-start.13 = (f32[34,1,128]{2,1,0:T(1,128)S(1)}, f32[34,1,128]{2,1,0:T(1,128)S(1)}, u32[]{:S(2)}, u32[]{:S(2)}) collective-permute-start(f32[34,1,128]{2,1,0:T(1,128)S(1)} %get-tuple-element.154), channel_id=1, source_target_pairs={{1,0},{2,1},{3,2},{4,3},{5,4},{6,5},{7,6},{8,7},{9,8},{10,9},{11,1... | collective-permute-start | bytes 52232 | tf_op jit(solution)/shard_map/ppermute | solution.py:21
  107.0 73.3 %collective-permute-start.30 = (f32[1,4,32]{2,1,0:T(4,128)S(1)}, f32[1,4,32]{2,1,0:T(4,128)S(1)}, u32[]{:S(2)}, u32[]{:S(2)}) collective-permute-start(f32[1,4,32]{2,1,0:T(4,128)S(1)} %get-tuple-element.248), channel_id=1, source_target_pairs={{0,16},{16,32},{32,48},{48,64},{64,80},{80,96},{96,112},{112,128},... | collective-permute-start | bytes 1544 | tf_op jit(solution)/shard_map/ppermute | solution.py:20
  107.1 76.2 %collective-permute-start.31 = (f32[1,4,32]{2,1,0:T(4,128)S(1)}, f32[1,4,32]{2,1,0:T(4,128)S(1)}, u32[]{:S(2)}, u32[]{:S(2)}) collective-permute-start(f32[1,4,32]{2,1,0:T(4,128)S(1)} %get-tuple-element.247), channel_id=1, source_target_pairs={{16,0},{32,16},{48,32},{64,48},{80,64},{96,80},{112,96},{128,112},... | collective-permute-start | bytes 1544 | tf_op jit(solution)/shard_map/ppermute | solution.py:21
  118.7 12.6 %collective-permute-start.16 = (f32[34,1,128]{2,1,0:T(1,128)S(1)}, f32[34,1,128]{2,1,0:T(1,128)S(1)}, u32[]{:S(2)}, u32[]{:S(2)}) collective-permute-start(f32[34,1,128]{2,1,0:T(1,128)S(1)} %get-tuple-element.151), channel_id=1, source_target_pairs={{0,1},{1,2},{2,3},{3,4},{4,5},{5,6},{6,7},{7,8},{8,9},{9,10},{10,1... | collective-permute-start | bytes 52232 | tf_op jit(solution)/shard_map/ppermute | solution.py:20
  122.0 11.3 %collective-permute-start.17 = (f32[34,1,128]{2,1,0:T(1,128)S(1)}, f32[34,1,128]{2,1,0:T(1,128)S(1)}, u32[]{:S(2)}, u32[]{:S(2)}) collective-permute-start(f32[34,1,128]{2,1,0:T(1,128)S(1)} %get-tuple-element.152), channel_id=1, source_target_pairs={{1,0},{2,1},{3,2},{4,3},{5,4},{6,5},{7,6},{8,7},{9,8},{10,9},{11,1... | collective-permute-start | bytes 52232 | tf_op jit(solution)/shard_map/ppermute | solution.py:21
  124.7 34.8 %collective-permute-start.20 = (f32[18,1,64]{2,1,0:T(1,128)S(1)}, f32[18,1,64]{2,1,0:T(1,128)S(1)}, u32[]{:S(2)}, u32[]{:S(2)}) collective-permute-start(f32[18,1,64]{2,1,0:T(1,128)S(1)} %get-tuple-element.192), channel_id=1, source_target_pairs={{0,1},{1,2},{2,3},{3,4},{4,5},{5,6},{6,7},{7,8},{8,9},{9,10},{10,1... | collective-permute-start | bytes 13832 | tf_op jit(solution)/shard_map/ppermute | solution.py:20
  131.4 28.2 %collective-permute-start.21 = (f32[18,1,64]{2,1,0:T(1,128)S(1)}, f32[18,1,64]{2,1,0:T(1,128)S(1)}, u32[]{:S(2)}, u32[]{:S(2)}) collective-permute-start(f32[18,1,64]{2,1,0:T(1,128)S(1)} %get-tuple-element.191), channel_id=1, source_target_pairs={{1,0},{2,1},{3,2},{4,3},{5,4},{6,5},{7,6},{8,7},{9,8},{10,9},{11,1... | collective-permute-start | bytes 13832 | tf_op jit(solution)/shard_map/ppermute | solution.py:21
  164.1 9.3 %collective-permute-start.24 = (f32[18,1,64]{2,1,0:T(1,128)S(1)}, f32[18,1,64]{2,1,0:T(1,128)S(1)}, u32[]{:S(2)}, u32[]{:S(2)}) collective-permute-start(f32[18,1,64]{2,1,0:T(1,128)S(1)} %get-tuple-element.189), channel_id=1, source_target_pairs={{0,1},{1,2},{2,3},{3,4},{4,5},{5,6},{6,7},{7,8},{8,9},{9,10},{10,1... | collective-permute-start | bytes 13832 | tf_op jit(solution)/shard_map/ppermute | solution.py:20
  171.3 8.9 %collective-permute-start.25 = (f32[18,1,64]{2,1,0:T(1,128)S(1)}, f32[18,1,64]{2,1,0:T(1,128)S(1)}, u32[]{:S(2)}, u32[]{:S(2)}) collective-permute-start(f32[18,1,64]{2,1,0:T(1,128)S(1)} %get-tuple-element.190), channel_id=1, source_target_pairs={{1,0},{2,1},{3,2},{4,3},{5,4},{6,5},{7,6},{8,7},{9,8},{10,9},{11,1... | collective-permute-start | bytes 13832 | tf_op jit(solution)/shard_map/ppermute | solution.py:21
  173.3 37.0 %collective-permute-start.42 = (f32[1,32,16]{1,2,0:T(8,128)}, f32[1,32,16]{1,2,0:T(8,128)}, u32[]{:S(2)}, u32[]{:S(2)}) collective-permute-start(f32[1,32,16]{1,2,0:T(8,128)} %get-tuple-element.217), channel_id=1, source_target_pairs={{0,16},{16,32},{32,48},{48,64},{64,80},{80,96},{96,112},{112,128},... | collective-permute-start | bytes 6152 | tf_op jit(solution)/shard_map/ppermute | solution.py:20
  173.3 37.0 %collective-permute-start.43 = (f32[1,32,16]{1,2,0:T(8,128)}, f32[1,32,16]{1,2,0:T(8,128)}, u32[]{:S(2)}, u32[]{:S(2)}) collective-permute-start(f32[1,32,16]{1,2,0:T(8,128)} %get-tuple-element.218), channel_id=1, source_target_pairs={{16,0},{32,16},{48,32},{64,48},{80,64},{96,80},{112,96},{128,112},... | collective-permute-start | bytes 6152 | tf_op jit(solution)/shard_map/ppermute | solution.py:21
  184.7 12.6 %collective-permute-start.28 = (f32[18,1,64]{2,1,0:T(1,128)S(1)}, f32[18,1,64]{2,1,0:T(1,128)S(1)}, u32[]{:S(2)}, u32[]{:S(2)}) collective-permute-start(f32[18,1,64]{2,1,0:T(1,128)S(1)} %get-tuple-element.187), channel_id=1, source_target_pairs={{0,1},{1,2},{2,3},{3,4},{4,5},{5,6},{6,7},{7,8},{8,9},{9,10},{10,1... | collective-permute-start | bytes 13832 | tf_op jit(solution)/shard_map/ppermute | solution.py:20
  188.0 11.4 %collective-permute-start.29 = (f32[18,1,64]{2,1,0:T(1,128)S(1)}, f32[18,1,64]{2,1,0:T(1,128)S(1)}, u32[]{:S(2)}, u32[]{:S(2)}) collective-permute-start(f32[18,1,64]{2,1,0:T(1,128)S(1)} %get-tuple-element.188), channel_id=1, source_target_pairs={{1,0},{2,1},{3,2},{4,3},{5,4},{6,5},{7,6},{8,7},{9,8},{10,9},{11,1... | collective-permute-start | bytes 13832 | tf_op jit(solution)/shard_map/ppermute | solution.py:21
  190.6 13.5 %collective-permute-start.32 = (f32[10,1,32]{2,1,0:T(1,128)}, f32[10,1,32]{2,1,0:T(1,128)}, u32[]{:S(2)}, u32[]{:S(2)}) collective-permute-start(f32[10,1,32]{2,1,0:T(1,128)} %get-tuple-element.228), channel_id=1, source_target_pairs={{0,1},{1,2},{2,3},{3,4},{4,5},{5,6},{6,7},{7,8},{8,9},{9,10},{10,1... | collective-permute-start | bytes 3848 | tf_op jit(solution)/shard_map/ppermute | solution.py:20
  197.3 9.1 %collective-permute-start.33 = (f32[10,1,32]{2,1,0:T(1,128)}, f32[10,1,32]{2,1,0:T(1,128)}, u32[]{:S(2)}, u32[]{:S(2)}) collective-permute-start(f32[10,1,32]{2,1,0:T(1,128)} %get-tuple-element.227), channel_id=1, source_target_pairs={{1,0},{2,1},{3,2},{4,3},{5,4},{6,5},{7,6},{8,7},{9,8},{10,9},{11,1... | collective-permute-start | bytes 3848 | tf_op jit(solution)/shard_map/ppermute | solution.py:21
  211.7 7.0 %collective-permute-start.36 = (f32[10,1,32]{2,1,0:T(1,128)S(1)}, f32[10,1,32]{2,1,0:T(1,128)S(1)}, u32[]{:S(2)}, u32[]{:S(2)}) collective-permute-start(f32[10,1,32]{2,1,0:T(1,128)S(1)} %get-tuple-element.225), channel_id=1, source_target_pairs={{0,1},{1,2},{2,3},{3,4},{4,5},{5,6},{6,7},{7,8},{8,9},{9,10},{10,1... | collective-permute-start | bytes 3848 | tf_op jit(solution)/shard_map/ppermute | solution.py:20
  216.6 8.8 %collective-permute-start.37 = (f32[10,1,32]{2,1,0:T(1,128)S(1)}, f32[10,1,32]{2,1,0:T(1,128)S(1)}, u32[]{:S(2)}, u32[]{:S(2)}) collective-permute-start(f32[10,1,32]{2,1,0:T(1,128)S(1)} %get-tuple-element.226), channel_id=1, source_target_pairs={{1,0},{2,1},{3,2},{4,3},{5,4},{6,5},{7,6},{8,7},{9,8},{10,9},{11,1... | collective-permute-start | bytes 3848 | tf_op jit(solution)/shard_map/ppermute | solution.py:21
  230.6 5.9 %collective-permute-start.40 = (f32[10,1,32]{2,1,0:T(1,128)S(1)}, f32[10,1,32]{2,1,0:T(1,128)S(1)}, u32[]{:S(2)}, u32[]{:S(2)}) collective-permute-start(f32[10,1,32]{2,1,0:T(1,128)S(1)} %get-tuple-element.223), channel_id=1, source_target_pairs={{0,1},{1,2},{2,3},{3,4},{4,5},{5,6},{6,7},{7,8},{8,9},{9,10},{10,1... | collective-permute-start | bytes 3848 | tf_op jit(solution)/shard_map/ppermute | solution.py:20
  232.5 8.8 %collective-permute-start.41 = (f32[10,1,32]{2,1,0:T(1,128)S(1)}, f32[10,1,32]{2,1,0:T(1,128)S(1)}, u32[]{:S(2)}, u32[]{:S(2)}) collective-permute-start(f32[10,1,32]{2,1,0:T(1,128)S(1)} %get-tuple-element.224), channel_id=1, source_target_pairs={{1,0},{2,1},{3,2},{4,3},{5,4},{6,5},{7,6},{8,7},{9,8},{10,9},{11,1... | collective-permute-start | bytes 3848 | tf_op jit(solution)/shard_map/ppermute | solution.py:21
  264.0 4.3 collective-permute-start.1
  268.5 4.3 collective-permute-start.1
  300.5 4.3 collective-permute-start.1
  305.1 4.3 collective-permute-start.1
  309.7 4.3 collective-permute-start.1
  337.2 6.9 %collective-permute-start.46 = (f32[10,1,32]{2,1,0:T(1,128)S(1)}, f32[10,1,32]{2,1,0:T(1,128)S(1)}, u32[]{:S(2)}, u32[]{:S(2)}) collective-permute-start(f32[10,1,32]{2,1,0:T(1,128)S(1)} %get-tuple-element.221), channel_id=1, source_target_pairs={{0,1},{1,2},{2,3},{3,4},{4,5},{5,6},{6,7},{7,8},{8,9},{9,10},{10,1... | collective-permute-start | bytes 3848 | tf_op jit(solution)/shard_map/ppermute | solution.py:20
  342.1 8.8 %collective-permute-start.47 = (f32[10,1,32]{2,1,0:T(1,128)S(1)}, f32[10,1,32]{2,1,0:T(1,128)S(1)}, u32[]{:S(2)}, u32[]{:S(2)}) collective-permute-start(f32[10,1,32]{2,1,0:T(1,128)S(1)} %get-tuple-element.222), channel_id=1, source_target_pairs={{1,0},{2,1},{3,2},{4,3},{5,4},{6,5},{7,6},{8,7},{9,8},{10,9},{11,1... | collective-permute-start | bytes 3848 | tf_op jit(solution)/shard_map/ppermute | solution.py:21
  356.0 5.9 %collective-permute-start.50 = (f32[10,1,32]{2,1,0:T(1,128)S(1)}, f32[10,1,32]{2,1,0:T(1,128)S(1)}, u32[]{:S(2)}, u32[]{:S(2)}) collective-permute-start(f32[10,1,32]{2,1,0:T(1,128)S(1)} %get-tuple-element.219), channel_id=1, source_target_pairs={{0,1},{1,2},{2,3},{3,4},{4,5},{5,6},{6,7},{7,8},{8,9},{9,10},{10,1... | collective-permute-start | bytes 3848 | tf_op jit(solution)/shard_map/ppermute | solution.py:20
  357.9 8.8 %collective-permute-start.51 = (f32[10,1,32]{2,1,0:T(1,128)S(1)}, f32[10,1,32]{2,1,0:T(1,128)S(1)}, u32[]{:S(2)}, u32[]{:S(2)}) collective-permute-start(f32[10,1,32]{2,1,0:T(1,128)S(1)} %get-tuple-element.220), channel_id=1, source_target_pairs={{1,0},{2,1},{3,2},{4,3},{5,4},{6,5},{7,6},{8,7},{9,8},{10,9},{11,1... | collective-permute-start | bytes 3848 | tf_op jit(solution)/shard_map/ppermute | solution.py:21
  372.3 5.9 %collective-permute-start.54 = (f32[18,1,64]{2,1,0:T(1,128)S(1)}, f32[18,1,64]{2,1,0:T(1,128)S(1)}, u32[]{:S(2)}, u32[]{:S(2)}) collective-permute-start(f32[18,1,64]{2,1,0:T(1,128)S(1)} %get-tuple-element.185), channel_id=1, source_target_pairs={{0,1},{1,2},{2,3},{3,4},{4,5},{5,6},{6,7},{7,8},{8,9},{9,10},{10,1... | collective-permute-start | bytes 13832 | tf_op jit(solution)/shard_map/ppermute | solution.py:20
  374.2 8.9 %collective-permute-start.55 = (f32[18,1,64]{2,1,0:T(1,128)S(1)}, f32[18,1,64]{2,1,0:T(1,128)S(1)}, u32[]{:S(2)}, u32[]{:S(2)}) collective-permute-start(f32[18,1,64]{2,1,0:T(1,128)S(1)} %get-tuple-element.186), channel_id=1, source_target_pairs={{1,0},{2,1},{3,2},{4,3},{5,4},{6,5},{7,6},{8,7},{9,8},{10,9},{11,1... | collective-permute-start | bytes 13832 | tf_op jit(solution)/shard_map/ppermute | solution.py:21
  388.5 5.9 %collective-permute-start.58 = (f32[18,1,64]{2,1,0:T(1,128)S(1)}, f32[18,1,64]{2,1,0:T(1,128)S(1)}, u32[]{:S(2)}, u32[]{:S(2)}) collective-permute-start(f32[18,1,64]{2,1,0:T(1,128)S(1)} %get-tuple-element.183), channel_id=1, source_target_pairs={{0,1},{1,2},{2,3},{3,4},{4,5},{5,6},{6,7},{7,8},{8,9},{9,10},{10,1... | collective-permute-start | bytes 13832 | tf_op jit(solution)/shard_map/ppermute | solution.py:20
  390.5 8.9 %collective-permute-start.59 = (f32[18,1,64]{2,1,0:T(1,128)S(1)}, f32[18,1,64]{2,1,0:T(1,128)S(1)}, u32[]{:S(2)}, u32[]{:S(2)}) collective-permute-start(f32[18,1,64]{2,1,0:T(1,128)S(1)} %get-tuple-element.184), channel_id=1, source_target_pairs={{1,0},{2,1},{3,2},{4,3},{5,4},{6,5},{7,6},{8,7},{9,8},{10,9},{11,1... | collective-permute-start | bytes 13832 | tf_op jit(solution)/shard_map/ppermute | solution.py:21
  405.8 6.0 %collective-permute-start.62 = (f32[34,1,128]{2,1,0:T(1,128)S(1)}, f32[34,1,128]{2,1,0:T(1,128)S(1)}, u32[]{:S(2)}, u32[]{:S(2)}) collective-permute-start(f32[34,1,128]{2,1,0:T(1,128)S(1)} %get-tuple-element.149), channel_id=1, source_target_pairs={{0,1},{1,2},{2,3},{3,4},{4,5},{5,6},{6,7},{7,8},{8,9},{9,10},{10,1... | collective-permute-start | bytes 52232 | tf_op jit(solution)/shard_map/ppermute | solution.py:20
  407.7 9.0 %collective-permute-start.63 = (f32[34,1,128]{2,1,0:T(1,128)S(1)}, f32[34,1,128]{2,1,0:T(1,128)S(1)}, u32[]{:S(2)}, u32[]{:S(2)}) collective-permute-start(f32[34,1,128]{2,1,0:T(1,128)S(1)} %get-tuple-element.150), channel_id=1, source_target_pairs={{1,0},{2,1},{3,2},{4,3},{5,4},{6,5},{7,6},{8,7},{9,8},{10,9},{11,1... | collective-permute-start | bytes 52232 | tf_op jit(solution)/shard_map/ppermute | solution.py:21
  421.5 6.0 %collective-permute-start.66 = (f32[34,1,128]{2,1,0:T(1,128)S(1)}, f32[34,1,128]{2,1,0:T(1,128)S(1)}, u32[]{:S(2)}, u32[]{:S(2)}) collective-permute-start(f32[34,1,128]{2,1,0:T(1,128)S(1)} %get-tuple-element.147), channel_id=1, source_target_pairs={{0,1},{1,2},{2,3},{3,4},{4,5},{5,6},{6,7},{7,8},{8,9},{9,10},{10,1... | collective-permute-start | bytes 52232 | tf_op jit(solution)/shard_map/ppermute | solution.py:20
  423.4 9.0 %collective-permute-start.67 = (f32[34,1,128]{2,1,0:T(1,128)S(1)}, f32[34,1,128]{2,1,0:T(1,128)S(1)}, u32[]{:S(2)}, u32[]{:S(2)}) collective-permute-start(f32[34,1,128]{2,1,0:T(1,128)S(1)} %get-tuple-element.148), channel_id=1, source_target_pairs={{1,0},{2,1},{3,2},{4,3},{5,4},{6,5},{7,6},{8,7},{9,8},{10,9},{11,1... | collective-permute-start | bytes 52232 | tf_op jit(solution)/shard_map/ppermute | solution.py:21
  (76 other events, 2063.8 us)
where the time goes:
time: 436 us; the launch traced here: 433 us
  starting transfers between devices  209 us (48%)
  waiting for transfers between devices  90.6 us (21%)
  local copies, waits for them, and re-layouts  49.2 us (11%)
  blocking collectives  41.7 us (10%)
  other arithmetic  40.7 us (9%)
    ppermute x48, starting transfers between devices, padded_2(): after = lax.ppermute(first, axis, down)  145 us
    ppermute x48, starting transfers between devices, padded_2(): before = lax.ppermute(last, axis, up)  64.2 us
    ppermute x48, waiting for transfers between devices, padded_2(): after = lax.ppermute(first, axis, down)  57.3 us
    reshape x4, local copies, waits for them, and re-layouts, coarsen(): field.reshape(size_x // 2, 2, size_y // 2, 2, size_z // 2, 2)  40.2 us
    ppermute x48, waiting for transfers between devices, padded_2(): before = lax.ppermute(last, axis, up)  33.3 us
    all_gather x1, blocking collectives, on_device(): lax.all_gather(coarse_perm, 'col', axis=1, tiled=True)  21.4 us
    all_gather x1, blocking collectives, on_device(): lax.all_gather(right_side, 'col', axis=1, tiled=True)  20.3 us
    reduce_sum x6, other arithmetic, coarsen(): field.reshape(size_x // 2, 2, size_y // 2, 2, size_z // 2, 2)  15.3 us
  transfers between devices with their start and end apart: 96, of which 39 were waited for; matrix products, arithmetic and copies ran while one was open for 18% of the time, Pallas kernels for 0%

commit v1 on v0

--- a/solution.py
+++ b/solution.py
@@ -8,6 +8,22 @@
 NU2 = 2
 CSWEEPS = 16
 OMEGA = 0.8
+
+
+def collect(x, axis, dim):
+    ways, here, step = (lax.axis_size(axis), lax.axis_index(axis), x.shape[dim])
+    dims = [n * ways if d == dim else n for d, n in enumerate(x.shape)]
+    full = lax.dynamic_update_slice_in_dim(jnp.zeros(dims, x.dtype), x, here * step, axis=dim)
+    going_up = going_down = x
+    for far in range(1, ways // 2 + 1):
+        going_up = lax.ppermute(going_up, axis, [(d, (d + 1) % ways) for d in range(ways)])
+        full = lax.dynamic_update_slice_in_dim(full, going_up, (here - far) % ways * step, axis=dim)
+        if 2 * far < ways:
+            going_down = lax.ppermute(going_down, axis, [(d, (d - 1) % ways) for d in range(ways)])
+            full = lax.dynamic_update_slice_in_dim(
+                full, going_down, (here + far) % ways * step, axis=dim
+            )
+    return full
 
 
 def padded_2(array, sides, width):
@@ -123,7 +139,7 @@
     size_x, size_y, size_z = right_side.shape
     coarse_scale = 0.25**LEVELS
     band_rhs, band_perm = (
-        lax.all_gather(right_side, "col", axis=1, tiled=True),
+        collect(right_side, "col", 1),
         lax.all_gather(coarse_perm, "col", axis=1, tiled=True),
     )
     band_faces = coefficients(band_perm_pad(band_perm), band_perm, coarse_scale)

time: 436 us -> 492 us (1.13)
  starting transfers between devices: 209 us -> 274 us
  blocking collectives: 41.7 us -> 21.4 us
  local copies, waits for them, and re-layouts: 49.2 us -> 60.5 us
    ppermute x0 -> x15, starting transfers between devices: none -> 66.1 us  [the longest x8 50.6 us: collect(): lax.ppermute(going_up, axis, [(d, (d + 1) % ways) for d in range(ways)])]
    all_gather x1 -> x0, blocking collectives: 20.3 us -> none  [on_device(): lax.all_gather(right_side, 'col', axis=1, tiled=True)]
    dynamic_update_slice x0 -> x16, local copies, waits for them, and re-layouts: none -> 11 us  [the longest x8 5.72 us: collect(): lax.dynamic_update_slice_in_dim(full, going_up, (here - far) % ways * ste...]
  transfers between devices with their start and end apart: 96 -> 111, of which waited for: 39 -> 39; matrix products, arithmetic and copies ran while one was open for 18% -> 18% of each run, Pallas kernels for 0% -> 0%
where the time goes in v1:
time: 492 us; the launch traced here: 490 us
  starting transfers between devices  274 us (56%)
  waiting for transfers between devices  90.7 us (18%)
  local copies, waits for them, and re-layouts  60.5 us (12%)
  other arithmetic  40.8 us (8%)
  blocking collectives  21.4 us (4%)
    ppermute x48, starting transfers between devices, padded_2(): after = lax.ppermute(first, axis, down)  146 us
    ppermute x48, starting transfers between devices, padded_2(): before = lax.ppermute(last, axis, up)  61.8 us
    ppermute x48, waiting for transfers between devices, padded_2(): after = lax.ppermute(first, axis, down)  55.9 us
    ppermute x8, starting transfers between devices, collect(): lax.ppermute(going_up, axis, [(d, (d + 1) % ways) for d in range(ways)])  50.6 us
    reshape x4, local copies, waits for them, and re-layouts, coarsen(): field.reshape(size_x // 2, 2, size_y // 2, 2, size_z // 2, 2)  40.2 us
    ppermute x48, waiting for transfers between devices, padded_2(): before = lax.ppermute(last, axis, up)  34.8 us
    all_gather x1, blocking collectives, on_device(): lax.all_gather(coarse_perm, 'col', axis=1, tiled=True)  21.4 us
    ppermute x7, starting transfers between devices, collect(): lax.ppermute(going_down, axis, [(d, (d - 1) % ways) for d in range(ways)])  15.4 us
  transfers between devices with their start and end apart: 111, of which 39 were waited for; matrix products, arithmetic and copies ran while one was open for 18% of the time, Pallas kernels for 0%

profile of v1, /device:TPU:30, one launch (start us, length us, event | category | flops | bytes accessed | tf_op | source)
XLA Modules:
  0.0 490.0 jit_solution(17432380541616120774)
XLA Ops:
  0.7 8.9 %collective-permute-start.3 = (f32[1,16,128]{2,1,0:T(8,128)S(1)}, f32[1,16,128]{2,1,0:T(8,128)S(1)}, u32[]{:S(2)}, u32[]{:S(2)}) collective-permute-start(f32[1,16,128]{2,1,0:T(8,128)S(1)} %get-tuple-element.167), channel_id=1, source_target_pairs={{16,0},{32,16},{48,32},{64,48},{80,64},{96,80},{112,96},{128,112},... | collective-permute-start | bytes 24584 | tf_op jit(solution)/shard_map/ppermute | solution.py:37
  10.4 3.0 collective-permute-start.7
  17.5 18.9 %reshape.48 = f32[16,2,8,2,64,2]{5,4,3,2,1,0:T(8,128)} reshape(f32[32,16,128]{2,1,0:T(8,128)} %param.7) | data formatting | bytes 524288 | tf_op jit(solution)/shard_map/reshape | solution.py:82
  36.4 7.0 %reduce_sum.55 = f32[16,8,64]{2,1,0:T(8,128)S(1)} reduce(f32[16,2,8,2,64,2]{5,4,3,2,1,0:T(8,128)} %reshape.48, f32[]{:T(128)} %constant.145.clone.1), dimensions={1,3,5}, to_apply=%region_1.0 | reduce | flops 57344 | bytes 294916 | tf_op jit(solution)/shard_map/reduce_sum | solution.py:82
  49.1 21.4 %all_gather.3 = f32[4,32,16]{2,0,1:T(4,128)S(1)} all-gather(f32[4,2,16]{2,0,1:T(4,128)S(1)} %copy.509), channel_id=1, replica_groups=mesh['row'=32,'col'=16] {'col'}, dimensions={1}, use_global_device_ids=true | all-gather | bytes 8704 | tf_op jit(solution)/shard_map/all_gather | solution.py:143
  72.6 4.6 collective-permute-start.4
  79.2 7.2 %collective-permute-start.8 = (f32[34,1,128]{2,1,0:T(1,128)S(1)}, f32[34,1,128]{2,1,0:T(1,128)S(1)}, u32[]{:S(2)}, u32[]{:S(2)}) collective-permute-start(f32[34,1,128]{2,1,0:T(1,128)S(1)} %get-tuple-element.147), channel_id=1, source_target_pairs={{0,1},{1,2},{2,3},{3,4},{4,5},{5,6},{6,7},{7,8},{8,9},{9,10},{10,1... | collective-permute-start | bytes 52232 | tf_op jit(solution)/shard_map/ppermute | solution.py:36
  91.4 4.0 collective-permute-done.9
  97.5 2.9 collective-permute-start.11
  101.9 3.2 collective-permute-start.12
  110.8 3.2 collective-permute-done.13
  119.5 3.3 collective-permute-start.16
  125.5 6.6 %collective-permute-start.20 = (f32[18,1,64]{2,1,0:T(1,128)S(1)}, f32[18,1,64]{2,1,0:T(1,128)S(1)}, u32[]{:S(2)}, u32[]{:S(2)}) collective-permute-start(f32[18,1,64]{2,1,0:T(1,128)S(1)} %get-tuple-element.182), channel_id=1, source_target_pairs={{0,1},{1,2},{2,3},{3,4},{4,5},{5,6},{6,7},{7,8},{8,9},{9,10},{10,1... | collective-permute-start | bytes 13832 | tf_op jit(solution)/shard_map/ppermute | solution.py:36
  135.2 18.1 %reshape.47 = f32[16,2,8,2,64,2]{5,4,3,2,1,0:T(8,128)} reshape(f32[32,16,128]{2,1,0:T(8,128)S(1)} %fusion.47) | data formatting | bytes 524288 | tf_op jit(solution)/shard_map/reshape | solution.py:82
  153.3 7.0 %reduce_sum.54 = f32[16,8,64]{2,1,0:T(8,128)S(1)} reduce(f32[16,2,8,2,64,2]{5,4,3,2,1,0:T(8,128)} %reshape.47, f32[]{:T(128)} %constant.145.clone.1), dimensions={1,3,5}, to_apply=%region_0.0 | reduce | flops 57344 | bytes 294916 | tf_op jit(solution)/shard_map/reduce_sum | solution.py:82
  160.6 2.9 collective-permute-start.23
  164.9 7.2 %collective-permute-start.24 = (f32[18,1,64]{2,1,0:T(1,128)S(1)}, f32[18,1,64]{2,1,0:T(1,128)S(1)}, u32[]{:S(2)}, u32[]{:S(2)}) collective-permute-start(f32[18,1,64]{2,1,0:T(1,128)S(1)} %get-tuple-element.179), channel_id=1, source_target_pairs={{0,1},{1,2},{2,3},{3,4},{4,5},{5,6},{6,7},{7,8},{8,9},{9,10},{10,1... | collective-permute-start | bytes 13832 | tf_op jit(solution)/shard_map/ppermute | solution.py:36
  174.2 2.9 collective-permute-start.58
  177.1 3.9 collective-permute-done.25
  185.5 3.3 collective-permute-start.28
  191.4 6.7 %collective-permute-start.32 = (f32[10,1,32]{2,1,0:T(1,128)}, f32[10,1,32]{2,1,0:T(1,128)}, u32[]{:S(2)}, u32[]{:S(2)}) collective-permute-start(f32[10,1,32]{2,1,0:T(1,128)} %get-tuple-element.218), channel_id=1, source_target_pairs={{0,1},{1,2},{2,3},{3,4},{4,5},{5,6},{6,7},{7,8},{8,9},{9,10},{10,1... | collective-permute-start | bytes 3848 | tf_op jit(solution)/shard_map/ppermute | solution.py:36
  201.1 3.0 reshape.49
  208.2 2.9 collective-permute-start.35
  212.5 4.9 %collective-permute-start.36 = (f32[10,1,32]{2,1,0:T(1,128)S(1)}, f32[10,1,32]{2,1,0:T(1,128)S(1)}, u32[]{:S(2)}, u32[]{:S(2)}) collective-permute-start(f32[10,1,32]{2,1,0:T(1,128)S(1)} %get-tuple-element.215), channel_id=1, source_target_pairs={{0,1},{1,2},{2,3},{3,4},{4,5},{5,6},{6,7},{7,8},{8,9},{9,10},{10,1... | collective-permute-start | bytes 3848 | tf_op jit(solution)/shard_map/ppermute | solution.py:36
  219.4 6.8 %collective-permute-done.37 = f32[10,1,32]{2,1,0:T(1,128)S(1)} collective-permute-done((f32[10,1,32]{2,1,0:T(1,128)S(1)}, f32[10,1,32]{2,1,0:T(1,128)S(1)}, u32[]{:S(2)}, u32[]{:S(2)}) %collective-permute-start.37) | collective-permute-done | bytes 1312 | tf_op jit(solution)/shard_map/ppermute | solution.py:37
  233.3 3.9 collective-permute-start.41
  237.3 4.8 collective-permute-done.41
  245.3 3.9 collective-permute-start.43
  249.2 5.2 %collective-permute-start.44 = (f32[4,2,16]{1,2,0:T(8,128)S(1)}, f32[4,2,16]{1,2,0:T(8,128)S(1)}, u32[]{:S(2)}, u32[]{:S(2)}) collective-permute-start(f32[4,2,16]{1,2,0:T(8,128)S(1)} %collective-permute-done.42), channel_id=1, source_target_pairs={{0,1},{1,2},{2,3},{3,4},{4,5},{5,6},{6,7},{7,8},{8,9},{9,10},{10,1... | collective-permute-start | bytes 1544 | tf_op jit(solution)/shard_map/ppermute | solution.py:19
  256.4 7.2 %collective-permute-start.46 = (f32[4,2,16]{1,2,0:T(8,128)S(1)}, f32[4,2,16]{1,2,0:T(8,128)S(1)}, u32[]{:S(2)}, u32[]{:S(2)}) collective-permute-start(f32[4,2,16]{1,2,0:T(8,128)S(1)} %collective-permute-done.44), channel_id=1, source_target_pairs={{0,1},{1,2},{2,3},{3,4},{4,5},{5,6},{6,7},{7,8},{8,9},{9,10},{10,1... | collective-permute-start | bytes 1544 | tf_op jit(solution)/shard_map/ppermute | solution.py:19
  265.6 7.2 %collective-permute-start.48 = (f32[4,2,16]{1,2,0:T(8,128)S(1)}, f32[4,2,16]{1,2,0:T(8,128)S(1)}, u32[]{:S(2)}, u32[]{:S(2)}) collective-permute-start(f32[4,2,16]{1,2,0:T(8,128)S(1)} %collective-permute-done.46), channel_id=1, source_target_pairs={{0,1},{1,2},{2,3},{3,4},{4,5},{5,6},{6,7},{7,8},{8,9},{9,10},{10,1... | collective-permute-start | bytes 1544 | tf_op jit(solution)/shard_map/ppermute | solution.py:19
  274.9 7.2 %collective-permute-start.50 = (f32[4,2,16]{1,2,0:T(8,128)S(1)}, f32[4,2,16]{1,2,0:T(8,128)S(1)}, u32[]{:S(2)}, u32[]{:S(2)}) collective-permute-start(f32[4,2,16]{1,2,0:T(8,128)S(1)} %collective-permute-done.48), channel_id=1, source_target_pairs={{0,1},{1,2},{2,3},{3,4},{4,5},{5,6},{6,7},{7,8},{8,9},{9,10},{10,1... | collective-permute-start | bytes 1544 | tf_op jit(solution)/shard_map/ppermute | solution.py:19
  284.1 7.2 %collective-permute-start.52 = (f32[4,2,16]{1,2,0:T(8,128)S(1)}, f32[4,2,16]{1,2,0:T(8,128)S(1)}, u32[]{:S(2)}, u32[]{:S(2)}) collective-permute-start(f32[4,2,16]{1,2,0:T(8,128)S(1)} %collective-permute-done.50), channel_id=1, source_target_pairs={{0,1},{1,2},{2,3},{3,4},{4,5},{5,6},{6,7},{7,8},{8,9},{9,10},{10,1... | collective-permute-start | bytes 1544 | tf_op jit(solution)/shard_map/ppermute | solution.py:19
  294.1 7.2 %collective-permute-start.54 = (f32[4,2,16]{1,2,0:T(8,128)S(1)}, f32[4,2,16]{1,2,0:T(8,128)S(1)}, u32[]{:S(2)}, u32[]{:S(2)}) collective-permute-start(f32[4,2,16]{1,2,0:T(8,128)S(1)} %collective-permute-done.52), channel_id=1, source_target_pairs={{0,1},{1,2},{2,3},{3,4},{4,5},{5,6},{6,7},{7,8},{8,9},{9,10},{10,1... | collective-permute-start | bytes 1544 | tf_op jit(solution)/shard_map/ppermute | solution.py:19
  307.2 7.2 %collective-permute-start.56 = (f32[4,2,16]{1,2,0:T(8,128)S(1)}, f32[4,2,16]{1,2,0:T(8,128)S(1)}, u32[]{:S(2)}, u32[]{:S(2)}) collective-permute-start(f32[4,2,16]{1,2,0:T(8,128)S(1)} %collective-permute-done.54), channel_id=1, source_target_pairs={{0,1},{1,2},{2,3},{3,4},{4,5},{5,6},{6,7},{7,8},{8,9},{9,10},{10,1... | collective-permute-start | bytes 1544 | tf_op jit(solution)/shard_map/ppermute | solution.py:19
  322.8 68.6 %while.10 = (s32[]{:T(128)}, f32[4,32,16]{1,2,0:T(8,128)S(1)}, f32[4,32,16]{1,2,0:T(8,128)S(1)}, f32[4,32,16]{1,2,0:T(8,128)S(1)}, f32[4,32,16]{1,2,0:T(8,128)S(...) while((s32[]{:T(128)}, f32[4,32,16]{1,2,0:T(8,128)S(1)}, ...), condition=%wide.region_7.8_spmd, body=%wide.region_6.7_spmd.sunk | while | flops 43010 | bytes 279997 | solution.py:113
  398.6 3.3 collective-permute-start.62
  402.0 5.5 %collective-permute-done.62 = f32[10,1,32]{2,1,0:T(1,128)S(1)} collective-permute-done((f32[10,1,32]{2,1,0:T(1,128)S(1)}, f32[10,1,32]{2,1,0:T(1,128)S(1)}, u32[]{:S(2)}, u32[]{:S(2)}) %collective-permute-start.62) | collective-permute-done | bytes 1312 | tf_op jit(solution)/shard_map/ppermute | solution.py:37
  414.5 3.9 collective-permute-start.66
  418.5 4.8 collective-permute-done.66
  430.8 3.9 collective-permute-start.70
  434.8 4.9 collective-permute-done.70
  447.0 3.9 collective-permute-start.74
  451.0 4.9 collective-permute-done.74
  464.3 3.9 collective-permute-start.78
  468.4 4.9 collective-permute-done.78
  480.0 3.9 collective-permute-start.82
  484.1 4.9 collective-permute-done.82
  (489 shorter events, 209.3 us)
Async XLA Ops:
  0.7 71.7 %collective-permute-start.2 = (f32[1,16,128]{2,1,0:T(8,128)S(1)}, f32[1,16,128]{2,1,0:T(8,128)S(1)}, u32[]{:S(2)}, u32[]{:S(2)}) collective-permute-start(f32[1,16,128]{2,1,0:T(8,128)S(1)} %get-tuple-element.168), channel_id=1, source_target_pairs={{0,16},{16,32},{32,48},{48,64},{64,80},{80,96},{96,112},{112,128},... | collective-permute-start | bytes 24584 | tf_op jit(solution)/shard_map/ppermute | solution.py:36
  0.7 71.8 %collective-permute-start.3 = (f32[1,16,128]{2,1,0:T(8,128)S(1)}, f32[1,16,128]{2,1,0:T(8,128)S(1)}, u32[]{:S(2)}, u32[]{:S(2)}) collective-permute-start(f32[1,16,128]{2,1,0:T(8,128)S(1)} %get-tuple-element.167), channel_id=1, source_target_pairs={{16,0},{32,16},{48,32},{64,48},{80,64},{96,80},{112,96},{128,112},... | collective-permute-start | bytes 24584 | tf_op jit(solution)/shard_map/ppermute | solution.py:37
  10.4 68.7 %collective-permute-start.6 = (f32[1,16,128]{2,1,0:T(8,128)S(1)}, f32[1,16,128]{2,1,0:T(8,128)S(1)}, u32[]{:S(2)}, u32[]{:S(2)}) collective-permute-start(f32[1,16,128]{2,1,0:T(8,128)S(1)} %get-tuple-element.172), channel_id=1, source_target_pairs={{0,16},{16,32},{32,48},{48,64},{64,80},{80,96},{96,112},{112,128},... | collective-permute-start | bytes 24584 | tf_op jit(solution)/shard_map/ppermute | solution.py:36
  10.4 68.8 %collective-permute-start.7 = (f32[1,16,128]{2,1,0:T(8,128)S(1)}, f32[1,16,128]{2,1,0:T(8,128)S(1)}, u32[]{:S(2)}, u32[]{:S(2)}) collective-permute-start(f32[1,16,128]{2,1,0:T(8,128)S(1)} %get-tuple-element.171), channel_id=1, source_target_pairs={{16,0},{32,16},{48,32},{64,48},{80,64},{96,80},{112,96},{128,112},... | collective-permute-start | bytes 24584 | tf_op jit(solution)/shard_map/ppermute | solution.py:37
  72.6 15.9 %collective-permute-start.4 = (f32[34,1,128]{2,1,0:T(1,128)S(1)}, f32[34,1,128]{2,1,0:T(1,128)S(1)}, u32[]{:S(2)}, u32[]{:S(2)}) collective-permute-start(f32[34,1,128]{2,1,0:T(1,128)S(1)} %get-tuple-element.146), channel_id=1, source_target_pairs={{0,1},{1,2},{2,3},{3,4},{4,5},{5,6},{6,7},{7,8},{8,9},{9,10},{10,1... | collective-permute-start | bytes 52232 | tf_op jit(solution)/shard_map/ppermute | solution.py:36
  77.2 14.2 %collective-permute-start.5 = (f32[34,1,128]{2,1,0:T(1,128)S(1)}, f32[34,1,128]{2,1,0:T(1,128)S(1)}, u32[]{:S(2)}, u32[]{:S(2)}) collective-permute-start(f32[34,1,128]{2,1,0:T(1,128)S(1)} %get-tuple-element.145), channel_id=1, source_target_pairs={{1,0},{2,1},{3,2},{4,3},{5,4},{6,5},{7,6},{8,7},{9,8},{10,9},{11,1... | collective-permute-start | bytes 52232 | tf_op jit(solution)/shard_map/ppermute | solution.py:37
  79.2 12.2 %collective-permute-start.8 = (f32[34,1,128]{2,1,0:T(1,128)S(1)}, f32[34,1,128]{2,1,0:T(1,128)S(1)}, u32[]{:S(2)}, u32[]{:S(2)}) collective-permute-start(f32[34,1,128]{2,1,0:T(1,128)S(1)} %get-tuple-element.147), channel_id=1, source_target_pairs={{0,1},{1,2},{2,3},{3,4},{4,5},{5,6},{6,7},{7,8},{8,9},{9,10},{10,1... | collective-permute-start | bytes 52232 | tf_op jit(solution)/shard_map/ppermute | solution.py:36
  86.5 9.0 %collective-permute-start.9 = (f32[34,1,128]{2,1,0:T(1,128)S(1)}, f32[34,1,128]{2,1,0:T(1,128)S(1)}, u32[]{:S(2)}, u32[]{:S(2)}) collective-permute-start(f32[34,1,128]{2,1,0:T(1,128)S(1)} %get-tuple-element.148), channel_id=1, source_target_pairs={{1,0},{2,1},{3,2},{4,3},{5,4},{6,5},{7,6},{8,7},{9,8},{10,9},{11,1... | collective-permute-start | bytes 52232 | tf_op jit(solution)/shard_map/ppermute | solution.py:37
  88.4 26.7 %collective-permute-start.18 = (f32[1,8,64]{2,1,0:T(8,128)S(1)}, f32[1,8,64]{2,1,0:T(8,128)S(1)}, u32[]{:S(2)}, u32[]{:S(2)}) collective-permute-start(f32[1,8,64]{2,1,0:T(8,128)S(1)} %get-tuple-element.202), channel_id=1, source_target_pairs={{0,16},{16,32},{32,48},{48,64},{64,80},{80,96},{96,112},{112,128},... | collective-permute-start | bytes 6152 | tf_op jit(solution)/shard_map/ppermute | solution.py:36
  88.5 29.7 %collective-permute-start.19 = (f32[1,8,64]{2,1,0:T(8,128)S(1)}, f32[1,8,64]{2,1,0:T(8,128)S(1)}, u32[]{:S(2)}, u32[]{:S(2)}) collective-permute-start(f32[1,8,64]{2,1,0:T(8,128)S(1)} %get-tuple-element.201), channel_id=1, source_target_pairs={{16,0},{32,16},{48,32},{64,48},{80,64},{96,80},{112,96},{128,112},... | collective-permute-start | bytes 6152 | tf_op jit(solution)/shard_map/ppermute | solution.py:37
  105.1 9.0 %collective-permute-start.13 = (f32[34,1,128]{2,1,0:T(1,128)S(1)}, f32[34,1,128]{2,1,0:T(1,128)S(1)}, u32[]{:S(2)}, u32[]{:S(2)}) collective-permute-start(f32[34,1,128]{2,1,0:T(1,128)S(1)} %get-tuple-element.144), channel_id=1, source_target_pairs={{1,0},{2,1},{3,2},{4,3},{5,4},{6,5},{7,6},{8,7},{9,8},{10,9},{11,1... | collective-permute-start | bytes 52232 | tf_op jit(solution)/shard_map/ppermute | solution.py:37
  107.9 73.3 %collective-permute-start.30 = (f32[1,4,32]{2,1,0:T(4,128)S(1)}, f32[1,4,32]{2,1,0:T(4,128)S(1)}, u32[]{:S(2)}, u32[]{:S(2)}) collective-permute-start(f32[1,4,32]{2,1,0:T(4,128)S(1)} %get-tuple-element.238), channel_id=1, source_target_pairs={{0,16},{16,32},{32,48},{48,64},{64,80},{80,96},{96,112},{112,128},... | collective-permute-start | bytes 1544 | tf_op jit(solution)/shard_map/ppermute | solution.py:36
  107.9 76.2 %collective-permute-start.31 = (f32[1,4,32]{2,1,0:T(4,128)S(1)}, f32[1,4,32]{2,1,0:T(4,128)S(1)}, u32[]{:S(2)}, u32[]{:S(2)}) collective-permute-start(f32[1,4,32]{2,1,0:T(4,128)S(1)} %get-tuple-element.237), channel_id=1, source_target_pairs={{16,0},{32,16},{48,32},{64,48},{80,64},{96,80},{112,96},{128,112},... | collective-permute-start | bytes 1544 | tf_op jit(solution)/shard_map/ppermute | solution.py:37
  119.5 12.6 %collective-permute-start.16 = (f32[34,1,128]{2,1,0:T(1,128)S(1)}, f32[34,1,128]{2,1,0:T(1,128)S(1)}, u32[]{:S(2)}, u32[]{:S(2)}) collective-permute-start(f32[34,1,128]{2,1,0:T(1,128)S(1)} %get-tuple-element.141), channel_id=1, source_target_pairs={{0,1},{1,2},{2,3},{3,4},{4,5},{5,6},{6,7},{7,8},{8,9},{9,10},{10,1... | collective-permute-start | bytes 52232 | tf_op jit(solution)/shard_map/ppermute | solution.py:36
  122.8 11.3 %collective-permute-start.17 = (f32[34,1,128]{2,1,0:T(1,128)S(1)}, f32[34,1,128]{2,1,0:T(1,128)S(1)}, u32[]{:S(2)}, u32[]{:S(2)}) collective-permute-start(f32[34,1,128]{2,1,0:T(1,128)S(1)} %get-tuple-element.142), channel_id=1, source_target_pairs={{1,0},{2,1},{3,2},{4,3},{5,4},{6,5},{7,6},{8,7},{9,8},{10,9},{11,1... | collective-permute-start | bytes 52232 | tf_op jit(solution)/shard_map/ppermute | solution.py:37
  125.5 34.8 %collective-permute-start.20 = (f32[18,1,64]{2,1,0:T(1,128)S(1)}, f32[18,1,64]{2,1,0:T(1,128)S(1)}, u32[]{:S(2)}, u32[]{:S(2)}) collective-permute-start(f32[18,1,64]{2,1,0:T(1,128)S(1)} %get-tuple-element.182), channel_id=1, source_target_pairs={{0,1},{1,2},{2,3},{3,4},{4,5},{5,6},{6,7},{7,8},{8,9},{9,10},{10,1... | collective-permute-start | bytes 13832 | tf_op jit(solution)/shard_map/ppermute | solution.py:36
  132.2 28.2 %collective-permute-start.21 = (f32[18,1,64]{2,1,0:T(1,128)S(1)}, f32[18,1,64]{2,1,0:T(1,128)S(1)}, u32[]{:S(2)}, u32[]{:S(2)}) collective-permute-start(f32[18,1,64]{2,1,0:T(1,128)S(1)} %get-tuple-element.181), channel_id=1, source_target_pairs={{1,0},{2,1},{3,2},{4,3},{5,4},{6,5},{7,6},{8,7},{9,8},{10,9},{11,1... | collective-permute-start | bytes 13832 | tf_op jit(solution)/shard_map/ppermute | solution.py:37
  164.9 9.3 %collective-permute-start.24 = (f32[18,1,64]{2,1,0:T(1,128)S(1)}, f32[18,1,64]{2,1,0:T(1,128)S(1)}, u32[]{:S(2)}, u32[]{:S(2)}) collective-permute-start(f32[18,1,64]{2,1,0:T(1,128)S(1)} %get-tuple-element.179), channel_id=1, source_target_pairs={{0,1},{1,2},{2,3},{3,4},{4,5},{5,6},{6,7},{7,8},{8,9},{9,10},{10,1... | collective-permute-start | bytes 13832 | tf_op jit(solution)/shard_map/ppermute | solution.py:36
  172.1 8.9 %collective-permute-start.25 = (f32[18,1,64]{2,1,0:T(1,128)S(1)}, f32[18,1,64]{2,1,0:T(1,128)S(1)}, u32[]{:S(2)}, u32[]{:S(2)}) collective-permute-start(f32[18,1,64]{2,1,0:T(1,128)S(1)} %get-tuple-element.180), channel_id=1, source_target_pairs={{1,0},{2,1},{3,2},{4,3},{5,4},{6,5},{7,6},{8,7},{9,8},{10,9},{11,1... | collective-permute-start | bytes 13832 | tf_op jit(solution)/shard_map/ppermute | solution.py:37
  174.1 117.2 %collective-permute-start.57 = (f32[1,32,16]{1,2,0:T(8,128)}, f32[1,32,16]{1,2,0:T(8,128)}, u32[]{:S(2)}, u32[]{:S(2)}) collective-permute-start(f32[1,32,16]{1,2,0:T(8,128)} %get-tuple-element.207), channel_id=1, source_target_pairs={{0,16},{16,32},{32,48},{48,64},{64,80},{80,96},{96,112},{112,128},... | collective-permute-start | bytes 6152 | tf_op jit(solution)/shard_map/ppermute | solution.py:36
  174.2 117.2 %collective-permute-start.58 = (f32[1,32,16]{1,2,0:T(8,128)}, f32[1,32,16]{1,2,0:T(8,128)}, u32[]{:S(2)}, u32[]{:S(2)}) collective-permute-start(f32[1,32,16]{1,2,0:T(8,128)} %get-tuple-element.208), channel_id=1, source_target_pairs={{16,0},{32,16},{48,32},{64,48},{80,64},{96,80},{112,96},{128,112},... | collective-permute-start | bytes 6152 | tf_op jit(solution)/shard_map/ppermute | solution.py:37
  185.5 12.6 %collective-permute-start.28 = (f32[18,1,64]{2,1,0:T(1,128)S(1)}, f32[18,1,64]{2,1,0:T(1,128)S(1)}, u32[]{:S(2)}, u32[]{:S(2)}) collective-permute-start(f32[18,1,64]{2,1,0:T(1,128)S(1)} %get-tuple-element.177), channel_id=1, source_target_pairs={{0,1},{1,2},{2,3},{3,4},{4,5},{5,6},{6,7},{7,8},{8,9},{9,10},{10,1... | collective-permute-start | bytes 13832 | tf_op jit(solution)/shard_map/ppermute | solution.py:36
  188.8 11.4 %collective-permute-start.29 = (f32[18,1,64]{2,1,0:T(1,128)S(1)}, f32[18,1,64]{2,1,0:T(1,128)S(1)}, u32[]{:S(2)}, u32[]{:S(2)}) collective-permute-start(f32[18,1,64]{2,1,0:T(1,128)S(1)} %get-tuple-element.178), channel_id=1, source_target_pairs={{1,0},{2,1},{3,2},{4,3},{5,4},{6,5},{7,6},{8,7},{9,8},{10,9},{11,1... | collective-permute-start | bytes 13832 | tf_op jit(solution)/shard_map/ppermute | solution.py:37
  191.4 13.5 %collective-permute-start.32 = (f32[10,1,32]{2,1,0:T(1,128)}, f32[10,1,32]{2,1,0:T(1,128)}, u32[]{:S(2)}, u32[]{:S(2)}) collective-permute-start(f32[10,1,32]{2,1,0:T(1,128)} %get-tuple-element.218), channel_id=1, source_target_pairs={{0,1},{1,2},{2,3},{3,4},{4,5},{5,6},{6,7},{7,8},{8,9},{9,10},{10,1... | collective-permute-start | bytes 3848 | tf_op jit(solution)/shard_map/ppermute | solution.py:36
  198.1 9.1 %collective-permute-start.33 = (f32[10,1,32]{2,1,0:T(1,128)}, f32[10,1,32]{2,1,0:T(1,128)}, u32[]{:S(2)}, u32[]{:S(2)}) collective-permute-start(f32[10,1,32]{2,1,0:T(1,128)} %get-tuple-element.217), channel_id=1, source_target_pairs={{1,0},{2,1},{3,2},{4,3},{5,4},{6,5},{7,6},{8,7},{9,8},{10,9},{11,1... | collective-permute-start | bytes 3848 | tf_op jit(solution)/shard_map/ppermute | solution.py:37
  212.5 7.0 %collective-permute-start.36 = (f32[10,1,32]{2,1,0:T(1,128)S(1)}, f32[10,1,32]{2,1,0:T(1,128)S(1)}, u32[]{:S(2)}, u32[]{:S(2)}) collective-permute-start(f32[10,1,32]{2,1,0:T(1,128)S(1)} %get-tuple-element.215), channel_id=1, source_target_pairs={{0,1},{1,2},{2,3},{3,4},{4,5},{5,6},{6,7},{7,8},{8,9},{9,10},{10,1... | collective-permute-start | bytes 3848 | tf_op jit(solution)/shard_map/ppermute | solution.py:36
  217.4 8.8 %collective-permute-start.37 = (f32[10,1,32]{2,1,0:T(1,128)S(1)}, f32[10,1,32]{2,1,0:T(1,128)S(1)}, u32[]{:S(2)}, u32[]{:S(2)}) collective-permute-start(f32[10,1,32]{2,1,0:T(1,128)S(1)} %get-tuple-element.216), channel_id=1, source_target_pairs={{1,0},{2,1},{3,2},{4,3},{5,4},{6,5},{7,6},{8,7},{9,8},{10,9},{11,1... | collective-permute-start | bytes 3848 | tf_op jit(solution)/shard_map/ppermute | solution.py:37
  233.3 8.8 %collective-permute-start.41 = (f32[10,1,32]{2,1,0:T(1,128)S(1)}, f32[10,1,32]{2,1,0:T(1,128)S(1)}, u32[]{:S(2)}, u32[]{:S(2)}) collective-permute-start(f32[10,1,32]{2,1,0:T(1,128)S(1)} %get-tuple-element.214), channel_id=1, source_target_pairs={{1,0},{2,1},{3,2},{4,3},{5,4},{6,5},{7,6},{8,7},{9,8},{10,9},{11,1... | collective-permute-start | bytes 3848 | tf_op jit(solution)/shard_map/ppermute | solution.py:37
  245.3 9.2 %collective-permute-start.43 = (f32[4,2,16]{1,2,0:T(8,128)S(1)}, f32[4,2,16]{1,2,0:T(8,128)S(1)}, u32[]{:S(2)}, u32[]{:S(2)}) collective-permute-start(f32[4,2,16]{1,2,0:T(8,128)S(1)} %broadcast_multiply_fusion.2), channel_id=1, source_target_pairs={{0,15},{1,0},{2,1},{3,2},{4,3},{5,4},{6,5},{7,6},{8,7},{9,8},{10,9... | collective-permute-start | bytes 1544 | tf_op jit(solution)/shard_map/ppermute | solution.py:22
  249.2 7.2 %collective-permute-start.44 = (f32[4,2,16]{1,2,0:T(8,128)S(1)}, f32[4,2,16]{1,2,0:T(8,128)S(1)}, u32[]{:S(2)}, u32[]{:S(2)}) collective-permute-start(f32[4,2,16]{1,2,0:T(8,128)S(1)} %collective-permute-done.42), channel_id=1, source_target_pairs={{0,1},{1,2},{2,3},{3,4},{4,5},{5,6},{6,7},{7,8},{8,9},{9,10},{10,1... | collective-permute-start | bytes 1544 | tf_op jit(solution)/shard_map/ppermute | solution.py:19
  254.5 9.2 %collective-permute-start.45 = (f32[4,2,16]{1,2,0:T(8,128)S(1)}, f32[4,2,16]{1,2,0:T(8,128)S(1)}, u32[]{:S(2)}, u32[]{:S(2)}) collective-permute-start(f32[4,2,16]{1,2,0:T(8,128)S(1)} %collective-permute-done.43), channel_id=1, source_target_pairs={{0,15},{1,0},{2,1},{3,2},{4,3},{5,4},{6,5},{7,6},{8,7},{9,8},{10,9... | collective-permute-start | bytes 1544 | tf_op jit(solution)/shard_map/ppermute | solution.py:22
  256.4 9.2 %collective-permute-start.46 = (f32[4,2,16]{1,2,0:T(8,128)S(1)}, f32[4,2,16]{1,2,0:T(8,128)S(1)}, u32[]{:S(2)}, u32[]{:S(2)}) collective-permute-start(f32[4,2,16]{1,2,0:T(8,128)S(1)} %collective-permute-done.44), channel_id=1, source_target_pairs={{0,1},{1,2},{2,3},{3,4},{4,5},{5,6},{6,7},{7,8},{8,9},{9,10},{10,1... | collective-permute-start | bytes 1544 | tf_op jit(solution)/shard_map/ppermute | solution.py:19
  263.7 9.2 %collective-permute-start.47 = (f32[4,2,16]{1,2,0:T(8,128)S(1)}, f32[4,2,16]{1,2,0:T(8,128)S(1)}, u32[]{:S(2)}, u32[]{:S(2)}) collective-permute-start(f32[4,2,16]{1,2,0:T(8,128)S(1)} %collective-permute-done.45), channel_id=1, source_target_pairs={{0,15},{1,0},{2,1},{3,2},{4,3},{5,4},{6,5},{7,6},{8,7},{9,8},{10,9... | collective-permute-start | bytes 1544 | tf_op jit(solution)/shard_map/ppermute | solution.py:22
  265.6 9.2 %collective-permute-start.48 = (f32[4,2,16]{1,2,0:T(8,128)S(1)}, f32[4,2,16]{1,2,0:T(8,128)S(1)}, u32[]{:S(2)}, u32[]{:S(2)}) collective-permute-start(f32[4,2,16]{1,2,0:T(8,128)S(1)} %collective-permute-done.46), channel_id=1, source_target_pairs={{0,1},{1,2},{2,3},{3,4},{4,5},{5,6},{6,7},{7,8},{8,9},{9,10},{10,1... | collective-permute-start | bytes 1544 | tf_op jit(solution)/shard_map/ppermute | solution.py:19
  272.9 9.2 %collective-permute-start.49 = (f32[4,2,16]{1,2,0:T(8,128)S(1)}, f32[4,2,16]{1,2,0:T(8,128)S(1)}, u32[]{:S(2)}, u32[]{:S(2)}) collective-permute-start(f32[4,2,16]{1,2,0:T(8,128)S(1)} %collective-permute-done.47), channel_id=1, source_target_pairs={{0,15},{1,0},{2,1},{3,2},{4,3},{5,4},{6,5},{7,6},{8,7},{9,8},{10,9... | collective-permute-start | bytes 1544 | tf_op jit(solution)/shard_map/ppermute | solution.py:22
  274.9 9.2 %collective-permute-start.50 = (f32[4,2,16]{1,2,0:T(8,128)S(1)}, f32[4,2,16]{1,2,0:T(8,128)S(1)}, u32[]{:S(2)}, u32[]{:S(2)}) collective-permute-start(f32[4,2,16]{1,2,0:T(8,128)S(1)} %collective-permute-done.48), channel_id=1, source_target_pairs={{0,1},{1,2},{2,3},{3,4},{4,5},{5,6},{6,7},{7,8},{8,9},{9,10},{10,1... | collective-permute-start | bytes 1544 | tf_op jit(solution)/shard_map/ppermute | solution.py:19
  282.2 10.0 %collective-permute-start.51 = (f32[4,2,16]{1,2,0:T(8,128)S(1)}, f32[4,2,16]{1,2,0:T(8,128)S(1)}, u32[]{:S(2)}, u32[]{:S(2)}) collective-permute-start(f32[4,2,16]{1,2,0:T(8,128)S(1)} %collective-permute-done.49), channel_id=1, source_target_pairs={{0,15},{1,0},{2,1},{3,2},{4,3},{5,4},{6,5},{7,6},{8,7},{9,8},{10,9... | collective-permute-start | bytes 1544 | tf_op jit(solution)/shard_map/ppermute | solution.py:22
  284.1 10.0 %collective-permute-start.52 = (f32[4,2,16]{1,2,0:T(8,128)S(1)}, f32[4,2,16]{1,2,0:T(8,128)S(1)}, u32[]{:S(2)}, u32[]{:S(2)}) collective-permute-start(f32[4,2,16]{1,2,0:T(8,128)S(1)} %collective-permute-done.50), channel_id=1, source_target_pairs={{0,1},{1,2},{2,3},{3,4},{4,5},{5,6},{6,7},{7,8},{8,9},{9,10},{10,1... | collective-permute-start | bytes 1544 | tf_op jit(solution)/shard_map/ppermute | solution.py:19
  292.2 13.1 %collective-permute-start.53 = (f32[4,2,16]{1,2,0:T(8,128)S(1)}, f32[4,2,16]{1,2,0:T(8,128)S(1)}, u32[]{:S(2)}, u32[]{:S(2)}) collective-permute-start(f32[4,2,16]{1,2,0:T(8,128)S(1)} %collective-permute-done.51), channel_id=1, source_target_pairs={{0,15},{1,0},{2,1},{3,2},{4,3},{5,4},{6,5},{7,6},{8,7},{9,8},{10,9... | collective-permute-start | bytes 1544 | tf_op jit(solution)/shard_map/ppermute | solution.py:22
  294.1 13.1 %collective-permute-start.54 = (f32[4,2,16]{1,2,0:T(8,128)S(1)}, f32[4,2,16]{1,2,0:T(8,128)S(1)}, u32[]{:S(2)}, u32[]{:S(2)}) collective-permute-start(f32[4,2,16]{1,2,0:T(8,128)S(1)} %collective-permute-done.52), channel_id=1, source_target_pairs={{0,1},{1,2},{2,3},{3,4},{4,5},{5,6},{6,7},{7,8},{8,9},{9,10},{10,1... | collective-permute-start | bytes 1544 | tf_op jit(solution)/shard_map/ppermute | solution.py:19
  305.3 14.9 %collective-permute-start.55 = (f32[4,2,16]{1,2,0:T(8,128)S(1)}, f32[4,2,16]{1,2,0:T(8,128)S(1)}, u32[]{:S(2)}, u32[]{:S(2)}) collective-permute-start(f32[4,2,16]{1,2,0:T(8,128)S(1)} %collective-permute-done.53), channel_id=1, source_target_pairs={{0,15},{1,0},{2,1},{3,2},{4,3},{5,4},{6,5},{7,6},{8,7},{9,8},{10,9... | collective-permute-start | bytes 1544 | tf_op jit(solution)/shard_map/ppermute | solution.py:22
  307.2 13.7 %collective-permute-start.56 = (f32[4,2,16]{1,2,0:T(8,128)S(1)}, f32[4,2,16]{1,2,0:T(8,128)S(1)}, u32[]{:S(2)}, u32[]{:S(2)}) collective-permute-start(f32[4,2,16]{1,2,0:T(8,128)S(1)} %collective-permute-done.54), channel_id=1, source_target_pairs={{0,1},{1,2},{2,3},{3,4},{4,5},{5,6},{6,7},{7,8},{8,9},{9,10},{10,1... | collective-permute-start | bytes 1544 | tf_op jit(solution)/shard_map/ppermute | solution.py:19
  398.6 8.8 %collective-permute-start.62 = (f32[10,1,32]{2,1,0:T(1,128)S(1)}, f32[10,1,32]{2,1,0:T(1,128)S(1)}, u32[]{:S(2)}, u32[]{:S(2)}) collective-permute-start(f32[10,1,32]{2,1,0:T(1,128)S(1)} %get-tuple-element.212), channel_id=1, source_target_pairs={{1,0},{2,1},{3,2},{4,3},{5,4},{6,5},{7,6},{8,7},{9,8},{10,9},{11,1... | collective-permute-start | bytes 3848 | tf_op jit(solution)/shard_map/ppermute | solution.py:37
  414.5 8.8 %collective-permute-start.66 = (f32[10,1,32]{2,1,0:T(1,128)S(1)}, f32[10,1,32]{2,1,0:T(1,128)S(1)}, u32[]{:S(2)}, u32[]{:S(2)}) collective-permute-start(f32[10,1,32]{2,1,0:T(1,128)S(1)} %get-tuple-element.210), channel_id=1, source_target_pairs={{1,0},{2,1},{3,2},{4,3},{5,4},{6,5},{7,6},{8,7},{9,8},{10,9},{11,1... | collective-permute-start | bytes 3848 | tf_op jit(solution)/shard_map/ppermute | solution.py:37
  430.8 8.9 %collective-permute-start.70 = (f32[18,1,64]{2,1,0:T(1,128)S(1)}, f32[18,1,64]{2,1,0:T(1,128)S(1)}, u32[]{:S(2)}, u32[]{:S(2)}) collective-permute-start(f32[18,1,64]{2,1,0:T(1,128)S(1)} %get-tuple-element.176), channel_id=1, source_target_pairs={{1,0},{2,1},{3,2},{4,3},{5,4},{6,5},{7,6},{8,7},{9,8},{10,9},{11,1... | collective-permute-start | bytes 13832 | tf_op jit(solution)/shard_map/ppermute | solution.py:37
  447.0 8.9 %collective-permute-start.74 = (f32[18,1,64]{2,1,0:T(1,128)S(1)}, f32[18,1,64]{2,1,0:T(1,128)S(1)}, u32[]{:S(2)}, u32[]{:S(2)}) collective-permute-start(f32[18,1,64]{2,1,0:T(1,128)S(1)} %get-tuple-element.174), channel_id=1, source_target_pairs={{1,0},{2,1},{3,2},{4,3},{5,4},{6,5},{7,6},{8,7},{9,8},{10,9},{11,1... | collective-permute-start | bytes 13832 | tf_op jit(solution)/shard_map/ppermute | solution.py:37
  464.3 9.0 %collective-permute-start.78 = (f32[34,1,128]{2,1,0:T(1,128)S(1)}, f32[34,1,128]{2,1,0:T(1,128)S(1)}, u32[]{:S(2)}, u32[]{:S(2)}) collective-permute-start(f32[34,1,128]{2,1,0:T(1,128)S(1)} %get-tuple-element.140), channel_id=1, source_target_pairs={{1,0},{2,1},{3,2},{4,3},{5,4},{6,5},{7,6},{8,7},{9,8},{10,9},{11,1... | collective-permute-start | bytes 52232 | tf_op jit(solution)/shard_map/ppermute | solution.py:37
  480.0 9.0 %collective-permute-start.82 = (f32[34,1,128]{2,1,0:T(1,128)S(1)}, f32[34,1,128]{2,1,0:T(1,128)S(1)}, u32[]{:S(2)}, u32[]{:S(2)}) collective-permute-start(f32[34,1,128]{2,1,0:T(1,128)S(1)} %get-tuple-element.138), channel_id=1, source_target_pairs={{1,0},{2,1},{3,2},{4,3},{5,4},{6,5},{7,6},{8,7},{9,8},{10,9},{11,1... | collective-permute-start | bytes 52232 | tf_op jit(solution)/shard_map/ppermute | solution.py:37
  (91 other events, 2347.6 us)
